TPU v7x, 512 devices: a whole 4x4x16 slice. The times are simulated.
512 devices in a mesh: blk: 16 (over x_hi, y, core), wide: 32 (over x_lo, z).
Axes of the slice: x: 4 (x_hi: 2, x_lo: 2; x = x_hi * 2 + x_lo), y: 4, z: 16, core: 2. Of those that a mesh axis runs over, the one named last changes fastest.
Arguments:
- series: bfloat16 [90112, 640], P(('blk', 'wide'))
- scrub_mask: int32 [640], replicated, may hold values from 0 to 1, as said below
- seed_index: int32 [4096], P(('blk', 'wide')), may hold values from 0 to 90111, as said below
Outputs:
- dispersion: bfloat16 [16, 5632, 4096], P(None, 'wide', 'blk')
- statistic: bfloat16 [16, 5632, 4096], P(None, 'wide', 'blk')
Inputs may be any that keep to these rules, and one draw needn't show every extreme that they name: Entry i of seed_index lies among the rows (i // 8) * 176 to (i // 8 + 1) * 176 - 1, and the 8 entries of one such block are distinct. `scrub_mask`: every frame of even position is kept.
All inputs are finite; a program needn't handle non-finite values.
Results may differ from a plain program's by a relative error of at most 0.0057.
Values may be sent and summed in bfloat16 or wider, within the bound.
No kernel may reach another device: no remote copies, remote signals or barrier semaphores. Data moves between devices by JAX's collectives and lax.ppermute only.
A program may use at most 128 MiB of HBM per device.

v0:
```python
import jax
import jax.numpy as jnp
from jax import lax
from jax.sharding import PartitionSpec as P

WIN = 60
STRIDE = 30
NWIN = 20
EPSILON = 1e-05
CLIP_LEVEL = 0.99


def fisher_of(values):
    clipped = jnp.clip(values, -CLIP_LEVEL, CLIP_LEVEL)
    return 0.5 * (jnp.log(1.0 + clipped) - jnp.log(1.0 - clipped))


def prepare(raw_rows, scrub_mask):
    values = raw_rows.astype(jnp.float32)
    row_count = values.shape[0]
    weight = scrub_mask.astype(jnp.float32)
    covered = STRIDE * (NWIN + 1)
    pieces = values[:, :covered].reshape(row_count, NWIN + 1, STRIDE)
    framed = jnp.concatenate([pieces[:, :-1], pieces[:, 1:]], axis=2)
    mask_pieces = weight[:covered].reshape(NWIN + 1, STRIDE)
    mask_framed = jnp.concatenate([mask_pieces[:-1], mask_pieces[1:]], axis=1)
    valid_count = jnp.sum(mask_framed, axis=1)
    centre = jnp.sum(framed * mask_framed, axis=2) / valid_count
    centred = (framed - centre[:, :, None]) * mask_framed
    spread = jnp.sum(centred * centred, axis=2)
    windows = (centred * lax.rsqrt(spread + EPSILON)[:, :, None]).astype(jnp.bfloat16)
    total_valid = jnp.sum(weight)
    mean_all = jnp.sum(values * weight, axis=1) / total_valid
    centred_all = (values - mean_all[:, None]) * weight
    spread_all = jnp.sum(centred_all * centred_all, axis=1)
    whole_std = (centred_all * lax.rsqrt(spread_all + EPSILON)[:, None]).astype(jnp.bfloat16)
    return (windows, whole_std)


def compare(target_windows, target_whole, seed_window, seed_whole, total_valid):
    window_corr = jnp.einsum(
        "tnw,snw->nts", target_windows, seed_window, preferred_element_type=jnp.float32
    )
    fisher = fisher_of(window_corr)
    first_moment = jnp.mean(fisher, axis=0)
    second = jnp.mean(fisher * fisher, axis=0)
    dispersion = ((WIN - 3) * (second - first_moment * first_moment)).astype(jnp.bfloat16)
    static = jnp.einsum("tf,sf->ts", target_whole, seed_whole, preferred_element_type=jnp.float32)
    statistic = (jnp.sqrt(total_valid - 3.0) * fisher_of(static)).astype(jnp.bfloat16)
    return (dispersion, statistic)


def body(series, scrub_mask, seed_index):
    row_count, frames = series.shape
    local_rows = seed_index % row_count
    own_seeds = jnp.take(series, local_rows, axis=0)
    total_valid = jnp.sum(scrub_mask.astype(jnp.float32))
    panel_rows = lax.all_gather(own_seeds, "wide", axis=0, tiled=True)
    seed_window, seed_whole = prepare(panel_rows, scrub_mask)
    blocks = lax.axis_size("blk")
    gathered = lax.all_gather(series, "blk", axis=0, tiled=True)
    target_windows, target_whole = prepare(gathered, scrub_mask)
    dispersion, statistic = compare(
        target_windows, target_whole, seed_window, seed_whole, total_valid
    )
    shape = (blocks, row_count, panel_rows.shape[0])
    return (dispersion.reshape(shape), statistic.reshape(shape))


def solution(mesh):
    in_specs = (P(("blk", "wide"), None), P(), P(("blk", "wide")))
    out_specs = (P(None, "wide", "blk"), P(None, "wide", "blk"))
    return jax.shard_map(body, mesh=mesh, in_specs=in_specs, out_specs=out_specs, check_vma=False)
```

profile of v0, /device:TPU:24, one launch (start us, length us, event | category | flops | bytes accessed | tf_op | source)
XLA Modules:
  0.0 186.0 jit_solution(18207394981131811877)
XLA Ops:
  7.2 0.0 all-gather.2.cloned.1.call-start
  7.2 0.7 all-gather.2.cloned.1.call-update
  7.9 0.7 convert_element_type.29
  8.6 1.3 convert_reduce_fusion
  10.6 0.7 compare_and_fusion
  11.3 1.5 gather_fusion
  12.8 0.1 fusion.17
  12.9 0.1 slice.44
  13.0 0.1 slice.46
  13.1 0.1 reduce_sum.132
  13.2 0.1 reduce_sum.133
  13.3 0.1 broadcast_select_fusion
  13.4 70.7 %all_gather.7 = bf16[256,640]{1,0:T(8,128)(2,1)S(1)} all-gather(bf16[8,640]{1,0:T(8,128)(2,1)S(1)} %broadcast_select_fusion), channel_id=1, replica_groups=mesh['blk'=16,'wide'=32] {'wide'}, dimensions={0}, use_global_device_ids=true | all-gather | bytes 337920 | tf_op jit(solution)/shard_map/all_gather | solution.py:58
  84.1 0.2 copy.10
  84.4 0.1 reshape.98
  84.5 0.1 pad_maximum_fusion.2
  84.5 0.1 multiply_reduce_fusion.8
  84.7 0.7 broadcast_divide_fusion.3
  85.3 0.2 multiply_reduce_fusion.7
  85.6 0.2 fusion.16
  85.7 0.3 multiply_reduce_fusion.6
  86.1 0.1 broadcast_divide_fusion.1
  86.2 0.5 multiply_reduce_fusion.5
  86.7 0.0 all-gather.2.cloned.1.call-done
  86.7 0.0 copy-start.2
  86.7 3.0 %multiply_reduce_fusion.4 = f32[2816]{0:T(1024)S(1)} fusion(bf16[2816,640]{1,0:T(8,128)(2,1)} %all-gather.2.cloned.1.call-done, f32[640]{0:T(1024)S(1)} %convert_element_type.29), kind=kLoop, calls=%fused_computation.13 | loop fusion | flops 5403904 | bytes 3618304 | tf_op jit(solution)/shard_map/reduce_sum | solution.py:33
  89.7 0.7 broadcast_divide_fusion.2
  90.3 3.8 %multiply_reduce_fusion.3 = f32[2816]{0:T(1024)S(1)} fusion(bf16[2816,640]{1,0:T(8,128)(2,1)} %all-gather.2.cloned.1.call-done, f32[2816]{0:T(1024)S(1)} %broadcast_divide_fusion.2, f32[640]{0:T(1024)S(1)} %convert_element_type.29), kind=kLoop, calls=%fused_computation.11 | loop fusion | flops 9008384 | bytes 3629568 | tf_op jit(solution)/shard_map/reduce_sum | solution.py:35
  94.1 0.0 copy-done.2
  94.1 3.4 %slice.52 = f32[2816,630]{1,0:T(8,128)} slice(bf16[2816,640]{1,0:T(8,128)(2,1)S(1)} %copy-done.2), slice={[0:2816], [0:630]} | slice | bytes 14192640 | tf_op jit(solution)/shard_map/slice | solution.py:23
  97.5 8.6 %copy.9 = f32[2816,630]{0,1:T(8,128)} copy(f32[2816,630]{1,0:T(8,128)} %slice.52) | data formatting | bytes 14192640 | tf_op jit(solution)/shard_map/slice | solution.py:23
  106.1 7.9 %reshape.97 = f32[2816,21,30]{0,2,1:T(8,128)} reshape(f32[2816,630]{0,1:T(8,128)} %copy.9) | data formatting | bytes 14192640 | tf_op jit(solution)/shard_map/reshape | solution.py:23
  114.0 11.9 %fusion.15 = (f32[2816,20,30]{0,2,1:T(8,128)}, f32[2816,20,30]{0,2,1:T(8,128)}) fusion(f32[2816,21,30]{0,2,1:T(8,128)} %reshape.97), kind=kLoop, calls=%fused_computation.54 | loop fusion | bytes 27033600 | tf_op jit(solution)/shard_map/slice | solution.py:24
  125.9 0.0 copy-start
  125.9 0.0 copy-start.1
  125.9 8.0 %multiply_reduce_fusion.2 = f32[2816,20]{0,1:T(8,128)S(1)} fusion(f32[2816,20,30]{0,2,1:T(8,128)} %get-tuple-element.7, f32[2816,20,30]{0,2,1:T(8,128)} %get-tuple-element.6, f32[20,60]{1,0:T(8,128)S(1)} %pad_maximum_fusion.2), kind=kLoop, calls=%fused_computation.8 | loop fusion | flops 10081280 | bytes 13746880 | tf_op jit(solution)/shard_map/reduce_sum | solution.py:28
  133.9 0.1 broadcast_divide_fusion
  134.0 0.0 copy-done
  134.0 1.2 copy-done.1
  135.3 3.5 %multiply_reduce_fusion.1 = f32[2816,20]{0,1:T(8,128)S(1)} fusion(f32[2816,20,30]{0,2,1:T(8,128)S(1)} %copy-done.1, f32[2816,20,30]{0,2,1:T(8,128)S(1)} %copy-done, f32[2816,20]{0,1:T(8,128)S(1)} %broadcast_divide_fusion, f32[20,60]{1,0:T(8,128)S(1)} %pad_maximum_fusion.2), kind=kLoop, calls=%fused_computation.6 | loop fusion | flops 16839680 | bytes 13972160 | tf_op jit(solution)/shard_map/reduce_sum | solution.py:30
  138.8 32.3 %multiply_reduce_fusion = (f32[2816,256]{1,0:T(8,128)}, f32[2816,256]{1,0:T(8,128)}) fusion(f32[256,20,30]{0,2,1:T(8,128)S(1)} %get-tuple-element.9, f32[256,20,30]{0,2,1:T(8,128)S(1)} %get-tuple-element.8, f32[256,20]{0,1:T(8,128)S(1)} %add_rsqrt_fusion.1, f32[256,20]{0,1:T(8,128)S(1)} %broadcast_divide_fusion.1, f32[20,60]{1,0:T(8,128)S(1)} %pad_maximum_fusion.2, ...), kind=kOutput, calls=%fused_computation.1 | convolution fusion | flops 1862483968 | bytes 21009088 | tf_op jit(solution)/shard_map/tnw,snw->nts/dot_general | solution.py:41
  171.1 0.0 copy-start.3
  171.1 4.5 %multiply_convert_fusion.7 = bf16[2816,256]{1,0:T(8,128)(2,1)} fusion(f32[2816,256]{1,0:T(8,128)} %get-tuple-element.3, f32[2816,256]{1,0:T(8,128)} %get-tuple-element.2), kind=kLoop, calls=%fused_computation.22 | loop fusion | flops 4325376 | bytes 7208960 | tf_op jit(solution)/shard_map/convert
  175.6 0.0 copy-done.3
  175.6 3.6 %multiply_convert_fusion.4 = bf16[2816,256]{1,0:T(8,128)(2,1)} fusion(bf16[2816,640]{1,0:T(8,128)(2,1)S(1)} %copy-done.3, f32[2816]{0:T(1024)S(1)} %add_rsqrt_fusion.2, f32[2816]{0:T(1024)S(1)} %broadcast_divide_fusion.2, f32[640]{0:T(1024)S(1)} %convert_element_type.29, f32[]{:T(128)S(6)} %mul.165, bf16[256,640]{1,0:T(8,128)(2,1)S(1)} %all_gather.7, ...), kind=kOutput, calls=%fused_computation.21 | convolution fusion | flops 936902656 | bytes 5401092 | tf_op jit(solution)/shard_map/tf,sf->ts/dot_general | solution.py:48
  (7 shorter events, 0.1 us)
Async XLA Ops:
  7.2 79.5 %all-gather.2.cloned.1.call-start = ((), (), s32[]{:S(2)}) async-start(), calls=%async_computation | async-start | bytes 3829760 | tf_op jit(solution)/shard_map/all_gather | solution.py:61
  86.7 7.4 %copy-start.2 = (bf16[2816,640]{1,0:T(8,128)(2,1)S(1)}, bf16[2816,640]{1,0:T(8,128)(2,1)}, u32[]{:S(2)}) copy-start(bf16[2816,640]{1,0:T(8,128)(2,1)} %all-gather.2.cloned.1.call-done) | copy-start | bytes 10813444
  125.9 8.1 %copy-start = (f32[2816,20,30]{0,2,1:T(8,128)S(1)}, f32[2816,20,30]{0,2,1:T(8,128)}, u32[]{:S(2)}) copy-start(f32[2816,20,30]{0,2,1:T(8,128)} %get-tuple-element.6) | copy-start | bytes 20275204
  125.9 9.4 %copy-start.1 = (f32[2816,20,30]{0,2,1:T(8,128)S(1)}, f32[2816,20,30]{0,2,1:T(8,128)}, u32[]{:S(2)}) copy-start(f32[2816,20,30]{0,2,1:T(8,128)} %get-tuple-element.7) | copy-start | bytes 20275204
  171.1 4.5 %copy-start.3 = (bf16[2816,640]{1,0:T(8,128)(2,1)S(1)}, bf16[2816,640]{1,0:T(8,128)(2,1)}, u32[]{:S(2)}) copy-start(bf16[2816,640]{1,0:T(8,128)(2,1)} %all-gather.2.cloned.1.call-done) | copy-start | bytes 10813444
Sparse Core Ops, SparseCore 0:
  11.2 71.5 all-gather.1
where the time goes:
time: 187 us; the launch traced here: 186 us
  blocking collectives  70.7 us (38%)
  matrix products  35.9 us (19%)
  local copies, waits for them, and re-layouts  35.3 us (19%)
  other arithmetic  28.5 us (15%)
  between operations  14.9 us (8%)
    all_gather x1, blocking collectives, body(): panel_rows = lax.all_gather(own_seeds, 'wide', axis=0, tiled=True)  70.7 us
    dot_general x1, matrix products, compare(): jnp.einsum('tnw,snw->nts', target_windows, seed_window, preferred_element...  32.3 us
    slice x4, local copies, waits for them, and re-layouts, prepare(): pieces = values[:, :covered].reshape(row_count, NWIN + 1, STRIDE)  12.3 us
    slice x2, local copies, waits for them, and re-layouts, prepare(): framed = jnp.concatenate([pieces[:, :-1], pieces[:, 1:]], axis=2)  12 us
    reduce_sum x2, other arithmetic, prepare(): centre = jnp.sum(framed * mask_framed, axis=2) / valid_count  8.33 us
    reshape x2, local copies, waits for them, and re-layouts, prepare(): pieces = values[:, :covered].reshape(row_count, NWIN + 1, STRIDE)  7.96 us
    another operation x1, other arithmetic  4.49 us
    reduce_sum x2, other arithmetic, prepare(): spread_all = jnp.sum(centred_all * centred_all, axis=1)  4.02 us
  transfers between devices with their start and end apart: 1, of which 0 were waited for; matrix products, arithmetic and copies ran while one was open for 4% of the time, Pallas kernels for 0%

commit v1 on v0

--- a/solution.py
+++ b/solution.py
@@ -1,3 +1,4 @@
+import functools
 import jax
 import jax.numpy as jnp
 from jax import lax
@@ -8,6 +9,15 @@
 NWIN = 20
 EPSILON = 1e-05
 CLIP_LEVEL = 0.99
+
+
+def lift_words(s0, axis_name):
+    then = jnp.stack(lax.axis_size(axis_name) * [s0], axis=0)
+    mat_out = lax.all_to_all(then, axis_name=axis_name, split_axis=0, concat_axis=0)
+    return jnp.concatenate(mat_out, axis=0)
+
+
+proceed_series = functools.partial(lift_words, axis_name="wide")
 
 
 def fisher_of(values):
@@ -55,7 +65,7 @@
     local_rows = seed_index % row_count
     own_seeds = jnp.take(series, local_rows, axis=0)
     total_valid = jnp.sum(scrub_mask.astype(jnp.float32))
-    panel_rows = lax.all_gather(own_seeds, "wide", axis=0, tiled=True)
+    panel_rows = proceed_series(own_seeds)
     seed_window, seed_whole = prepare(panel_rows, scrub_mask)
     blocks = lax.axis_size("blk")
     gathered = lax.all_gather(series, "blk", axis=0, tiled=True)

time: 187 us -> 185 us (0.989)
  blocking collectives: 70.7 us -> 0 us
  waiting for transfers between devices: 0.7 us -> 50.4 us
  starting transfers between devices: 0.04 us -> 16.4 us
    all_gather x1 -> x0, blocking collectives: 70.7 us -> none  [body(): panel_rows = lax.all_gather(own_seeds, 'wide', axis=0, tiled=True)]
    all_gather x1, waiting for transfers between devices: 0.02 us -> 28.2 us  [body(): gathered = lax.all_gather(series, 'blk', axis=0, tiled=True)]
    all_to_all x0 -> x1, waiting for transfers between devices: none -> 21.6 us  [lift_words(): lax.all_to_all(then, axis_name=axis_name, split_axis=0, concat_axis=0)]
    all_to_all x0 -> x1, starting transfers between devices: none -> 16.4 us  [lift_words(): lax.all_to_all(then, axis_name=axis_name, split_axis=0, concat_axis=0)]
    slice x4 -> x3, local copies, waits for them, and re-layouts: 12.3 us -> 12.2 us  [prepare(): pieces = values[:, :covered].reshape(row_count, NWIN + 1, STRIDE)]
  transfers between devices with their start and end apart: 1 -> 2, of which waited for: 0 -> 2; matrix products, arithmetic and copies ran while one was open for 4% -> 4% of each run, Pallas kernels for 0% -> 0%
where the time goes in v1:
time: 185 us; the launch traced here: 182 us
  waiting for transfers between devices  50.4 us (27%)
  local copies, waits for them, and re-layouts  36.2 us (20%)
  matrix products  36.1 us (20%)
  other arithmetic  28.3 us (15%)
  starting transfers between devices  16.4 us (9%)
  between operations  14.9 us (8%)
    dot_general x1, matrix products, compare(): jnp.einsum('tnw,snw->nts', target_windows, seed_window, preferred_element...  32.5 us
    all_gather x1, waiting for transfers between devices, body(): gathered = lax.all_gather(series, 'blk', axis=0, tiled=True)  28.2 us
    all_to_all x1, waiting for transfers between devices, lift_words(): lax.all_to_all(then, axis_name=axis_name, split_axis=0, concat_axis=0)  21.6 us
    all_to_all x1, starting transfers between devices, lift_words(): lax.all_to_all(then, axis_name=axis_name, split_axis=0, concat_axis=0)  16.4 us
    slice x3, local copies, waits for them, and re-layouts, prepare(): pieces = values[:, :covered].reshape(row_count, NWIN + 1, STRIDE)  12.2 us
    slice x2, local copies, waits for them, and re-layouts, prepare(): framed = jnp.concatenate([pieces[:, :-1], pieces[:, 1:]], axis=2)  12 us
    reduce_sum x2, other arithmetic, prepare(): centre = jnp.sum(framed * mask_framed, axis=2) / valid_count  8.32 us
    reshape x2, local copies, waits for them, and re-layouts, prepare(): pieces = values[:, :covered].reshape(row_count, NWIN + 1, STRIDE)  7.96 us
  transfers between devices with their start and end apart: 2, of which 2 were waited for; matrix products, arithmetic and copies ran while one was open for 4% of the time, Pallas kernels for 0%

profile of v1, /device:TPU:24, one launch (start us, length us, event | category | flops | bytes accessed | tf_op | source)
XLA Modules:
  0.0 182.3 jit_solution(16849584445205467434)
XLA Ops:
  7.2 0.0 all-gather.2.cloned.1.call-start
  7.2 0.7 all-gather.2.cloned.1.call-update
  7.9 0.7 compare_and_fusion
  8.6 1.5 gather_fusion
  10.1 0.1 broadcast_select_fusion
  10.2 0.8 stack.2
  11.0 16.4 %all-to-all-start = ((bf16[32,8,640]{2,1,0:T(8,128)(2,1)}), bf16[32,8,640]{2,1,0:T(8,128)(2,1)S(1)}, u32[]{:S(2)}, u32[]{:S(2)}) async-start(bf16[32,8,640]{2,1,0:T(8,128)(2,1)} %stack.2), calls=%async_computation | async-start | bytes 655360 | tf_op jit(solution)/shard_map/all_to_all | solution.py:16
  27.4 0.7 convert_element_type.36
  28.1 1.3 convert_reduce_fusion
  30.1 0.1 fusion.21
  30.1 0.1 slice.44
  30.2 0.1 slice.46
  30.3 0.1 reduce_sum.132
  30.4 0.1 reduce_sum.133
  30.5 0.1 pad_maximum_fusion.2
  30.6 21.6 %all-to-all-done = bf16[32,8,640]{2,1,0:T(8,128)(2,1)S(1)} async-done(((bf16[32,8,640]{2,1,0:T(8,128)(2,1)}), bf16[32,8,640]{2,1,0:T(8,128)(2,1)S(1)}, u32[]{:S(2)}, u32[]{:S(2)}) %all-to-all-start) | async-done | bytes 327712 | tf_op jit(solution)/shard_map/all_to_all | solution.py:16
  52.2 0.1 fusion.8
  52.3 0.7 broadcast_divide_fusion.2
  53.0 0.1 div.64
  53.1 0.2 fusion.11
  53.3 0.1 rsqrt.35
  53.5 0.2 copy.12
  53.7 0.1 reshape.135
  53.8 0.1 fusion.20
  54.0 0.3 multiply_reduce_fusion.6
  54.3 0.1 broadcast_divide_fusion.1
  54.4 0.5 multiply_reduce_fusion.5
  54.9 28.2 %all-gather.2.cloned.1.call-done = bf16[2816,640]{1,0:T(8,128)(2,1)} async-done(((bf16[176,640]{1,0:T(8,128)(2,1)}), bf16[2816,640]{1,0:T(8,128)(2,1)}) %all-gather.2.cloned.1.call-update) | async-done | bytes 3604496 | tf_op jit(solution)/shard_map/all_gather | solution.py:71
  83.0 0.0 copy-start.2
  83.0 2.9 %multiply_reduce_fusion.4 = f32[2816]{0:T(1024)S(1)} fusion(bf16[2816,640]{1,0:T(8,128)(2,1)} %all-gather.2.cloned.1.call-done, f32[640]{0:T(1024)S(1)} %convert_element_type.36), kind=kLoop, calls=%fused_computation.13 | loop fusion | flops 5403904 | bytes 3618304 | tf_op jit(solution)/shard_map/reduce_sum | solution.py:43
  86.0 0.7 broadcast_divide_fusion.3
  86.7 3.6 %multiply_reduce_fusion.3 = f32[2816]{0:T(1024)S(1)} fusion(bf16[2816,640]{1,0:T(8,128)(2,1)} %all-gather.2.cloned.1.call-done, f32[2816]{0:T(1024)S(1)} %broadcast_divide_fusion.3, f32[640]{0:T(1024)S(1)} %convert_element_type.36), kind=kLoop, calls=%fused_computation.11 | loop fusion | flops 9008384 | bytes 3629568 | tf_op jit(solution)/shard_map/reduce_sum | solution.py:45
  90.3 0.0 copy-done.2
  90.3 3.4 %slice.52 = f32[2816,630]{1,0:T(8,128)} slice(bf16[2816,640]{1,0:T(8,128)(2,1)S(1)} %copy-done.2), slice={[0:2816], [0:630]} | slice | bytes 14192640 | tf_op jit(solution)/shard_map/slice | solution.py:33
  93.7 8.6 %copy.11 = f32[2816,630]{0,1:T(8,128)} copy(f32[2816,630]{1,0:T(8,128)} %slice.52) | data formatting | bytes 14192640 | tf_op jit(solution)/shard_map/slice | solution.py:33
  102.3 7.9 %reshape.134 = f32[2816,21,30]{0,2,1:T(8,128)} reshape(f32[2816,630]{0,1:T(8,128)} %copy.11) | data formatting | bytes 14192640 | tf_op jit(solution)/shard_map/reshape | solution.py:33
  110.2 11.9 %fusion.19 = (f32[2816,20,30]{0,2,1:T(8,128)}, f32[2816,20,30]{0,2,1:T(8,128)}) fusion(f32[2816,21,30]{0,2,1:T(8,128)} %reshape.134), kind=kLoop, calls=%fused_computation.58 | loop fusion | bytes 27033600 | tf_op jit(solution)/shard_map/slice | solution.py:34
  122.1 0.0 copy-start
  122.1 0.0 copy-start.1
  122.1 8.0 %multiply_reduce_fusion.2 = f32[2816,20]{0,1:T(8,128)S(1)} fusion(f32[2816,20,30]{0,2,1:T(8,128)} %get-tuple-element.7, f32[2816,20,30]{0,2,1:T(8,128)} %get-tuple-element.6, f32[20,60]{1,0:T(8,128)S(1)} %pad_maximum_fusion.2), kind=kLoop, calls=%fused_computation.8 | loop fusion | flops 10081280 | bytes 13746880 | tf_op jit(solution)/shard_map/reduce_sum | solution.py:38
  130.1 0.1 broadcast_divide_fusion
  130.2 0.0 copy-done
  130.2 1.2 copy-done.1
  131.4 3.5 %multiply_reduce_fusion.1 = f32[2816,20]{0,1:T(8,128)S(1)} fusion(f32[2816,20,30]{0,2,1:T(8,128)S(1)} %copy-done.1, f32[2816,20,30]{0,2,1:T(8,128)S(1)} %copy-done, f32[2816,20]{0,1:T(8,128)S(1)} %broadcast_divide_fusion, f32[20,60]{1,0:T(8,128)S(1)} %pad_maximum_fusion.2), kind=kLoop, calls=%fused_computation.6 | loop fusion | flops 16839680 | bytes 13972160 | tf_op jit(solution)/shard_map/reduce_sum | solution.py:40
  134.9 32.5 %multiply_reduce_fusion = (f32[2816,256]{1,0:T(8,128)}, f32[2816,256]{1,0:T(8,128)}) fusion(f32[256,20,30]{0,2,1:T(8,128)S(1)} %get-tuple-element.9, f32[256,20,30]{0,2,1:T(8,128)S(1)} %get-tuple-element.8, f32[256,20]{0,1:T(8,128)S(1)} %add_rsqrt_fusion.1, f32[256,20]{0,1:T(8,128)S(1)} %broadcast_divide_fusion.1, f32[20,60]{1,0:T(8,128)S(1)} %pad_maximum_fusion.2, ...), kind=kOutput, calls=%fused_computation.1 | convolution fusion | flops 1862483968 | bytes 21009088 | tf_op jit(solution)/shard_map/tnw,snw->nts/dot_general | solution.py:51
  167.4 4.5 %multiply_convert_fusion.7 = bf16[2816,256]{1,0:T(8,128)(2,1)} fusion(f32[2816,256]{1,0:T(8,128)} %get-tuple-element.3, f32[2816,256]{1,0:T(8,128)} %get-tuple-element.2), kind=kLoop, calls=%fused_computation.22 | loop fusion | flops 4325376 | bytes 7208960 | tf_op jit(solution)/shard_map/convert.1
  171.9 0.0 copy-done.3
  171.9 3.6 %multiply_convert_fusion.4 = bf16[2816,256]{1,0:T(8,128)(2,1)} fusion(bf16[2816,640]{1,0:T(8,128)(2,1)S(1)} %copy-done.3, f32[2816]{0:T(1024)S(1)} %add_rsqrt_fusion.3, f32[2816]{0:T(1024)S(1)} %broadcast_divide_fusion.3, f32[640]{0:T(1024)S(1)} %convert_element_type.36, f32[]{:T(128)S(6)} %mul.174, f32[256]{0:T(256)S(1)} %rsqrt.35, f32[256]{0:T(256)S(1)} %div.64, ...), kind=kOutput, calls=%fused_computation.21 | convolution fusion | flops 936902656 | bytes 5401092 | tf_op jit(solution)/shard_map/tf,sf->ts/dot_general | solution.py:58
  (8 shorter events, 0.1 us)
Async XLA Ops:
  7.2 75.9 %all-gather.2.cloned.1.call-start = ((), (), s32[]{:S(2)}) async-start(), calls=%async_computation.1 | async-start | bytes 3829760 | tf_op jit(solution)/shard_map/all_gather | solution.py:71
  11.0 41.2 %all-to-all-start = ((bf16[32,8,640]{2,1,0:T(8,128)(2,1)}), bf16[32,8,640]{2,1,0:T(8,128)(2,1)S(1)}, u32[]{:S(2)}, u32[]{:S(2)}) async-start(bf16[32,8,640]{2,1,0:T(8,128)(2,1)} %stack.2), calls=%async_computation | async-start | bytes 655360 | tf_op jit(solution)/shard_map/all_to_all | solution.py:16
  83.0 7.2 %copy-start.2 = (bf16[2816,640]{1,0:T(8,128)(2,1)S(1)}, bf16[2816,640]{1,0:T(8,128)(2,1)}, u32[]{:S(2)}) copy-start(bf16[2816,640]{1,0:T(8,128)(2,1)} %all-gather.2.cloned.1.call-done) | copy-start | bytes 10813444
  122.1 8.1 %copy-start = (f32[2816,20,30]{0,2,1:T(8,128)S(1)}, f32[2816,20,30]{0,2,1:T(8,128)}, u32[]{:S(2)}) copy-start(f32[2816,20,30]{0,2,1:T(8,128)} %get-tuple-element.6) | copy-start | bytes 20275204
  122.1 9.4 %copy-start.1 = (f32[2816,20,30]{0,2,1:T(8,128)S(1)}, f32[2816,20,30]{0,2,1:T(8,128)}, u32[]{:S(2)}) copy-start(f32[2816,20,30]{0,2,1:T(8,128)} %get-tuple-element.7) | copy-start | bytes 20275204
  167.4 4.5 %copy-start.3 = (bf16[2816,640]{1,0:T(8,128)(2,1)S(1)}, bf16[2816,640]{1,0:T(8,128)(2,1)}, u32[]{:S(2)}) copy-start(bf16[2816,640]{1,0:T(8,128)(2,1)} %all-gather.2.cloned.1.call-done) | copy-start | bytes 10813444
Sparse Core Ops, SparseCore 0:
  11.2 71.7 all-gather.1
